TPU v7x, 32 devices: a whole 2x2x4 slice. The times are simulated.
32 devices in a mesh: grp: 4 (over x, core), rel: 8 (over z, y).
Axes of the slice: x: 2, y: 2, z: 4, core: 2. Of those that a mesh axis runs over, the one named last changes fastest.
Arguments:
- head_ids: int32 [65536], P(('grp', 'rel')), may hold values from 0 to 1023
- relations: int32 [65536, 1], P(('grp', 'rel')), may hold values from 0 to 31; in each aligned block of 2048 rows (0 to 2047, 2048 to 4095, ...) at most 128 rows name the same one
- tail_ids: int32 [65536], P(('grp', 'rel')), may hold values from 0 to 1023
- neg_owner: int32 [1], replicated, may hold values from 0 to 31
- entities: bfloat16 [32768, 512], P(('grp', 'rel')), may hold values from -0.3984375 to 0.3984375
- rel_weight: float32 [32, 512, 512], P('rel'), may hold values from -6 to 6
- rel_accum: float32 [32, 512], P('rel'), may hold values from 0.001 to 0.1
Outputs:
- losses: bfloat16 [65536], P(('grp', 'rel'))
- head_grad: bfloat16 [65536, 512], P(('grp', 'rel'))
- new_rel: float32 [32, 512, 512], P('rel')
- new_accum: float32 [32, 512], P('rel')
Inputs may be any that keep to these rules, and one draw needn't show every extreme that they name: `head_ids`: a row of the device's own shard of 1024 entity rows. `tail_ids`: a row of the device's own shard of 1024 entity rows. `relations`: in the 2048 rows of one device no relation is named by more than 128 rows; some relation is named by exactly 128. `neg_owner`: a device index, counted grp first, then rel.
All inputs are finite; a program needn't handle non-finite values.
Results may differ from a plain program's by a relative error of at most 0.0095.
Values may be sent and summed in bfloat16 or wider, within the bound.
No kernel may reach another device: no remote copies, remote signals or barrier semaphores. Data moves between devices by JAX's collectives and lax.ppermute only.
A program may use at most 128 MiB of HBM per device.

v0:
```python
import jax
import jax.numpy as jnp
from jax import lax
from jax.sharding import PartitionSpec as P

LEARNING_RATE = 1.0


def broadcast(shard, axis, root):
    mine = lax.axis_index(axis) == root
    return lax.psum(jnp.where(mine, shard, jnp.zeros_like(shard)), axis)


def slot_ranks(rel_ids, bucket_count):
    one_hot = (rel_ids[..., None] == jnp.arange(bucket_count, dtype=jnp.int32)).astype(jnp.int32)
    running = jnp.cumsum(one_hot, axis=-2) - 1
    return jnp.sum(one_hot * running, axis=-1)


def score_rows(query_rows, tail_rows, negatives):
    positive = jnp.sum(query_rows.astype(jnp.float32) * tail_rows.astype(jnp.float32), axis=-1)
    neg_scores = jnp.dot(query_rows, negatives.T, preferred_element_type=jnp.float32)
    losses = jax.nn.softplus(-positive) + jnp.mean(jax.nn.softplus(neg_scores), axis=-1)
    coefs = (jax.nn.sigmoid(neg_scores) / negatives.shape[0]).astype(jnp.bfloat16)
    grad_query = -jax.nn.sigmoid(-positive)[:, None] * tail_rows.astype(jnp.float32)
    grad_query = grad_query + jnp.dot(coefs, negatives, preferred_element_type=jnp.float32)
    return (losses.astype(jnp.bfloat16), grad_query.astype(jnp.bfloat16))


def adagrad(weight, accumulator, gradient):
    new_accum = accumulator + jnp.mean(gradient * gradient, axis=-1)
    return (weight - LEARNING_RATE * gradient / jnp.sqrt(new_accum)[..., None], new_accum)


def to_buckets(values, position, layout):
    flat_shape = (layout[0] * layout[1] * layout[2],) + values.shape[1:]
    filled = jnp.zeros(flat_shape, values.dtype).at[position].set(values)
    return filled.reshape(layout + values.shape[1:])


def from_buckets(stacked, position):
    return stacked.reshape((-1,) + stacked.shape[3:])[position]


def per_device(head_ids, relations, tail_ids, neg_owner, entities, rel_weight, rel_accum):
    rows_here = head_ids.shape[0]
    width = entities.shape[1]
    owner_count = lax.axis_size("rel")
    local_rels = rel_weight.shape[0]
    capacity = 2 * rows_here // (owner_count * local_rels)
    layout = (owner_count, local_rels, capacity)
    rel_ids = relations[:, 0]
    position = rel_ids * capacity + slot_ranks(rel_ids, owner_count * local_rels)
    head_rows = jnp.take(entities, head_ids, axis=0)
    tail_rows = jnp.take(entities, tail_ids, axis=0)
    matrices = rel_weight.astype(jnp.bfloat16)
    negatives = broadcast(entities, ("grp", "rel"), neg_owner[0])
    held_rows, held_tails = (
        lax.all_to_all(
            to_buckets(head_rows, position, layout), "rel", split_axis=0, concat_axis=0, tiled=True
        ),
        lax.all_to_all(
            to_buckets(tail_rows, position, layout), "rel", split_axis=0, concat_axis=0, tiled=True
        ),
    )
    projected = jnp.einsum(
        "srcd,rde->srce", held_rows, matrices, preferred_element_type=jnp.float32
    ).astype(jnp.bfloat16)
    slot_losses, slot_grads = score_rows(
        projected.reshape(-1, width), held_tails.reshape(-1, width), negatives
    )
    grad_rows = slot_grads.reshape(held_rows.shape)
    partial_value = jnp.einsum(
        "srcd,srce->rde", held_rows, grad_rows, preferred_element_type=jnp.float32
    )
    head_back = jnp.einsum(
        "srce,rde->srcd", grad_rows, matrices, preferred_element_type=jnp.float32
    ).astype(jnp.bfloat16)
    partial_value, head_back = (partial_value, head_back)
    back_grads, back_losses = (
        lax.all_to_all(head_back, "rel", split_axis=0, concat_axis=0, tiled=True),
        lax.all_to_all(slot_losses.reshape(layout), "rel", split_axis=0, concat_axis=0, tiled=True),
    )
    head_grad = from_buckets(back_grads, position)
    losses = from_buckets(back_losses, position)
    summed = lax.psum(partial_value.astype(jnp.bfloat16), "grp").astype(jnp.float32)
    new_rel, new_accum = adagrad(rel_weight, rel_accum, summed)
    return (losses, head_grad, new_rel, new_accum)


def solution(mesh):
    placed = (
        P(("grp", "rel")),
        P(("grp", "rel"), None),
        P(("grp", "rel")),
        P(),
        P(("grp", "rel"), None),
        P("rel", None, None),
        P("rel", None),
    )
    return jax.shard_map(
        per_device,
        mesh=mesh,
        in_specs=placed,
        out_specs=(
            P(("grp", "rel")),
            P(("grp", "rel"), None),
            P("rel", None, None),
            P("rel", None),
        ),
        check_vma=False,
    )
```

profile of v0, /device:TPU:0, one launch (start us, length us, event | category | flops | bytes accessed | tf_op | source)
XLA Modules:
  0.0 504.7 jit_solution(10861121189316165478)
XLA Ops:
  7.2 0.7 compare_and_fusion
  7.9 0.7 fusion.34
  8.6 0.7 fusion.30
  9.3 9.1 %reduce-window.6 = s32[32,16,128]{2,1,0:T(8,128)S(1)} reduce-window(s32[32,16,128]{2,1,0:T(8,128)S(1)} %fusion.30, s32[]{:T(128)} %constant.22.clone.1), window={size=1x1x128 pad=0_0x0_0x127_0}, to_apply=%region_0.0 | reduce-window | flops 8323072 | bytes 524292 | tf_op jit(solution)/shard_map/reduce-window
  18.4 0.1 slice.16
  18.5 0.2 copy.60
  18.7 0.2 reduce-window.9
  18.9 0.1 add_add_fusion
  19.1 0.8 fusion.29
  19.9 0.7 compare_select_fusion.1
  20.6 27.7 %scatter_custom_fusion.1 = bf16[4096,512]{1,0:T(8,128)(2,1)} fusion(s32[2048]{0:T(1024)S(1)} %bitcast.69, bf16[]{:T(256)} %constant.20.clone.1, pred[2048]{0:T(1024)(128)(4,1)S(1)} %compare_and_fusion, bf16[]{:T(256)} %constant.15.clone.2, bf16[1024,512]{1,0:T(8,128)(2,1)} %param.13, s32[2048]{0:T(1024)S(1)} %fusion.34), kind=kCustom, calls=%fused_computation.28 | custom fusion | flops 1048576 | bytes 5253124 | tf_op jit(solution)/shard_map/scatter | solution.py:37
  48.3 0.0 copy-start.2
  48.3 0.0 copy-start
  48.3 7.4 %all-to-all-start.1 = ((bf16[8,4,128,512]{3,2,1,0:T(8,128)(2,1)}), bf16[8,4,128,512]{3,2,1,0:T(8,128)(2,1)}, u32[]{:S(2)}, u32[]{:S(2)}) async-start(bf16[8,4,128,512]{3,2,1,0:T(8,128)(2,1)} %bitcast.60), calls=%async_computation.1 | async-start | bytes 8388608 | tf_op jit(solution)/shard_map/all_to_all | solution.py:62
  55.7 0.0 copy-done.2
  55.8 0.0 copy-done
  55.8 22.6 %scatter_custom_fusion = bf16[4096,512]{1,0:T(8,128)(2,1)} fusion(s32[2048]{0:T(1024)S(1)} %bitcast.70, bf16[]{:T(256)} %constant.20.clone.1, pred[2048]{0:T(1024)(128)(4,1)S(1)} %compare_and_fusion.1, bf16[]{:T(256)} %constant.15.clone.2, bf16[1024,512]{1,0:T(8,128)(2,1)S(1)} %copy-done, s32[2048]{0:T(1024)S(1)} %fusion.33), kind=kCustom, calls=%fused_computation.30 | custom fusion | flops 1048576 | bytes 5253124 | tf_op jit(solution)/shard_map/scatter | solution.py:37
  78.4 70.6 %all-to-all-done.1 = bf16[8,4,128,512]{3,2,1,0:T(8,128)(2,1)} async-done(((bf16[8,4,128,512]{3,2,1,0:T(8,128)(2,1)}), bf16[8,4,128,512]{3,2,1,0:T(8,128)(2,1)}, u32[]{:S(2)}, u32[]{:S(2)}) %all-to-all-start.1) | async-done | bytes 4194336 | tf_op jit(solution)/shard_map/all_to_all | solution.py:62
  149.0 4.6 all-to-all-start
  153.6 0.3 all-reduce.3.cloned.1.call-start
  154.6 1.0 broadcast_select_fusion
  155.6 0.0 all-reduce.3.cloned.1.call-update
  155.6 95.5 %all-to-all-done = bf16[8,4,128,512]{3,2,1,0:T(8,128)(2,1)} async-done(((bf16[8,4,128,512]{3,2,1,0:T(8,128)(2,1)}), bf16[8,4,128,512]{3,2,1,0:T(8,128)(2,1)}, u32[]{:S(2)}, u32[]{:S(2)}) %all-to-all-start) | async-done | bytes 4194336 | tf_op jit(solution)/shard_map/all_to_all | solution.py:59
  251.2 7.2 %multiply_reduce_fusion = (f32[8,4,128]{2,0,1:T(8,128)S(1)}, bf16[8,4,128,512]{3,2,0,1:T(8,128)(2,1)S(1)}) fusion(bf16[8,4,128,512]{3,2,1,0:T(8,128)(2,1)} %all-to-all-done.1, f32[4,512,512]{2,1,0:T(8,128)} %param.14, bf16[8,4,128,512]{3,2,1,0:T(8,128)(2,1)} %all-to-all-done), kind=kOutput, calls=%fused_computation.12 | convolution fusion | flops 2159013888 | bytes 16793600 | tf_op jit(solution)/shard_map/srcd,rde->srce/dot_general | solution.py:66
  258.3 2.5 copy.50
  260.8 3.4 copy_convert_fusion
  264.2 4.2 copy.54
  268.4 82.8 %all-reduce.3.cloned.1.call-done = bf16[1024,512]{1,0:T(8,128)(2,1)} async-done(((bf16[1024,512]{1,0:T(8,128)(2,1)}), bf16[1024,512]{1,0:T(8,128)(2,1)}) %all-reduce.3.cloned.1.call-update) | async-done | bytes 1048592 | tf_op jit(solution)/shard_map/psum | solution.py:11
  351.2 0.0 copy-start.4
  351.3 16.5 %fusion = (f32[4096]{0:T(1024)S(1)}, f32[4096,1024]{0,1:T(8,128)}) fusion(bf16[4096,512]{1,0:T(8,128)(2,1)} %bitcast.61, bf16[1024,512]{1,0:T(8,128)(2,1)} %all-reduce.3.cloned.1.call-done), kind=kOutput, calls=%fused_computation.7 | convolution fusion | flops 4324323328 | bytes 22036480 | tf_op jit(solution)/shard_map/dot_general | solution.py:22
  367.8 0.6 copy.52
  368.4 4.4 all-to-all-start.2
  372.8 0.0 copy-done.4
  372.8 0.0 copy-start.1
  372.8 11.3 %fusion.2 = bf16[4096,512]{1,0:T(8,128)(2,1)S(1)} fusion(f32[8,4,128,512]{3,2,1,0:T(8,128)} %copy.54, bf16[1024,512]{1,0:T(8,128)(2,1)S(1)} %copy-done.4, f32[4096,1024]{0,1:T(8,128)} %get-tuple-element.12, f32[4096]{0:T(1024)S(1)} %bitcast.72), kind=kOutput, calls=%fused_computation.11 | convolution fusion | flops 4322230272 | bytes 30425088 | tf_op jit(solution)/shard_map/dot_general | solution.py:26
  384.2 0.0 copy-start.5
  384.2 0.0 copy-done.1
  384.2 2.4 convert_bitcast_fusion
  386.6 0.0 copy-done.5
  386.6 2.2 copy.56
  388.8 0.0 all-to-all-done.2
  388.8 6.0 %all-to-all-start.3 = ((bf16[8,4,128,512]{3,2,1,0:T(8,128)(2,1)}), bf16[8,4,128,512]{3,2,1,0:T(8,128)(2,1)}, u32[]{:S(2)}, u32[]{:S(2)}) async-start(bf16[8,4,128,512]{3,2,1,0:T(8,128)(2,1)} %copy.56), calls=%async_computation.3 | async-start | bytes 8388608 | tf_op jit(solution)/shard_map/all_to_all | solution.py:81
  394.8 0.0 all-reduce.5.cloned.1.call-start
  394.9 7.2 %bitcast_convert_fusion = bf16[4,512,512]{2,1,0:T(8,128)(2,1)} fusion(bf16[8,4,128,512]{3,2,1,0:T(8,128)(2,1)} %all-to-all-done, bf16[8,4,128,512]{3,2,1,0:T(8,128)(2,1)} %bitcast.74), kind=kOutput, calls=%fused_computation.18 | convolution fusion | flops 2148532224 | bytes 10485760 | tf_op jit(solution)/shard_map/srcd,srce->rde/dot_general | solution.py:73
  402.0 0.0 copy-start.3
  402.0 0.0 all-reduce.5.cloned.1.call-update
  402.1 22.1 %gather_fusion = bf16[2048]{0:T(1024)(128)(2,1)} fusion(bf16[4096]{0:T(1024)(128)(2,1)S(1)} %bitcast.58, s32[2048]{0:T(1024)S(1)} %broadcast_clamp_fusion), kind=kCustom, calls=%fused_computation.2 | custom fusion | bytes 16384 | tf_op jit(solution)/shard_map/gather | solution.py:42
  424.2 29.9 %all-reduce.5.cloned.1.call-done = bf16[4,512,512]{2,1,0:T(8,128)(2,1)} async-done(((bf16[4,512,512]{2,1,0:T(8,128)(2,1)}), bf16[4,512,512]{2,1,0:T(8,128)(2,1)}) %all-reduce.5.cloned.1.call-update) | async-done | bytes 2097168 | tf_op jit(solution)/shard_map/psum | solution.py:86
  454.1 2.1 fusion.4
  456.2 0.0 copy-done.3
  456.2 0.6 fusion.39
  456.8 5.5 %fusion.5 = f32[4,512,512]{2,1,0:T(8,128)} fusion(f32[4,512,512]{2,1,0:T(8,128)} %param.14, bf16[4,512,512]{2,1,0:T(8,128)(2,1)} %all-reduce.5.cloned.1.call-done, f32[4,512]{1,0:T(4,128)S(1)} %get-tuple-element.5), kind=kLoop, calls=%fused_computation.17 | loop fusion | flops 3145728 | bytes 10493952 | tf_op jit(solution)/shard_map/sub | solution.py:32
  462.3 23.6 %all-to-all-done.3 = bf16[8,4,128,512]{3,2,1,0:T(8,128)(2,1)} async-done(((bf16[8,4,128,512]{3,2,1,0:T(8,128)(2,1)}), bf16[8,4,128,512]{3,2,1,0:T(8,128)(2,1)}, u32[]{:S(2)}, u32[]{:S(2)}) %all-to-all-start.3) | async-done | bytes 4194336 | tf_op jit(solution)/shard_map/all_to_all | solution.py:81
  485.9 12.0 %gather_fusion.1 = bf16[2048,512]{1,0:T(8,128)(2,1)} fusion(bf16[4096,512]{1,0:T(8,128)(2,1)} %bitcast.21, s32[2048]{0:T(1024)S(1)} %broadcast_clamp_fusion), kind=kCustom, calls=%fused_computation.3 | custom fusion | bytes 4202496 | tf_op jit(solution)/shard_map/gather | solution.py:42
  (6 shorter events, 0.1 us)
Async XLA Ops:
  48.3 7.4 %copy-start.2 = (s32[2048]{0:T(1024)S(1)}, s32[2048]{0:T(1024)}, u32[]{:S(2)}) copy-start(s32[2048]{0:T(1024)} %param.9) | copy-start | bytes 24580
  48.3 7.5 %copy-start = (bf16[1024,512]{1,0:T(8,128)(2,1)S(1)}, bf16[1024,512]{1,0:T(8,128)(2,1)}, u32[]{:S(2)}) copy-start(bf16[1024,512]{1,0:T(8,128)(2,1)} %param.13) | copy-start | bytes 3145732
  48.3 100.7 %all-to-all-start.1 = ((bf16[8,4,128,512]{3,2,1,0:T(8,128)(2,1)}), bf16[8,4,128,512]{3,2,1,0:T(8,128)(2,1)}, u32[]{:S(2)}, u32[]{:S(2)}) async-start(bf16[8,4,128,512]{3,2,1,0:T(8,128)(2,1)} %bitcast.60), calls=%async_computation.1 | async-start | bytes 8388608 | tf_op jit(solution)/shard_map/all_to_all | solution.py:62
  149.0 102.1 %all-to-all-start = ((bf16[8,4,128,512]{3,2,1,0:T(8,128)(2,1)}), bf16[8,4,128,512]{3,2,1,0:T(8,128)(2,1)}, u32[]{:S(2)}, u32[]{:S(2)}) async-start(bf16[8,4,128,512]{3,2,1,0:T(8,128)(2,1)} %bitcast.59), calls=%async_computation | async-start | bytes 8388608 | tf_op jit(solution)/shard_map/all_to_all | solution.py:59
  153.6 197.6 %all-reduce.3.cloned.1.call-start = ((), (), s32[]{:S(2)}) async-start(), calls=%async_computation.4 | async-start | bytes 2097152 | tf_op jit(solution)/shard_map/psum | solution.py:11
  351.2 21.6 %copy-start.4 = (bf16[1024,512]{1,0:T(8,128)(2,1)S(1)}, bf16[1024,512]{1,0:T(8,128)(2,1)}, u32[]{:S(2)}) copy-start(bf16[1024,512]{1,0:T(8,128)(2,1)} %all-reduce.3.cloned.1.call-done) | copy-start | bytes 3145732
  368.4 20.4 %all-to-all-start.2 = ((bf16[8,4,128]{2,1,0:T(4,128)(2,1)}), bf16[8,4,128]{2,1,0:T(4,128)(2,1)S(1)}, u32[]{:S(2)}, u32[]{:S(2)}) async-start(bf16[8,4,128]{2,1,0:T(4,128)(2,1)} %copy.52), calls=%async_computation.2 | async-start | bytes 16384 | tf_op jit(solution)/shard_map/all_to_all | solution.py:82
  372.8 11.3 %copy-start.1 = (f32[4,512,512]{2,1,0:T(8,128)S(1)}, f32[4,512,512]{2,1,0:T(8,128)}, u32[]{:S(2)}) copy-start(f32[4,512,512]{2,1,0:T(8,128)} %param.14) | copy-start | bytes 12582916
  384.2 2.4 copy-start.5
  388.8 97.0 %all-to-all-start.3 = ((bf16[8,4,128,512]{3,2,1,0:T(8,128)(2,1)}), bf16[8,4,128,512]{3,2,1,0:T(8,128)(2,1)}, u32[]{:S(2)}, u32[]{:S(2)}) async-start(bf16[8,4,128,512]{3,2,1,0:T(8,128)(2,1)} %copy.56), calls=%async_computation.3 | async-start | bytes 8388608 | tf_op jit(solution)/shard_map/all_to_all | solution.py:81
  394.8 59.3 %all-reduce.5.cloned.1.call-start = ((), (), s32[]{:S(2)}) async-start(), calls=%async_computation.5 | async-start | bytes 4194304 | tf_op jit(solution)/shard_map/psum | solution.py:86
  402.0 54.1 %copy-start.3 = (f32[4,512]{1,0:T(4,128)S(1)}, f32[4,512]{1,0:T(4,128)}, u32[]{:S(2)}) copy-start(f32[4,512]{1,0:T(4,128)} %param.15) | copy-start | bytes 24580
Sparse Core Ops, SparseCore 0:
  160.2 190.9 all-reduce.2
  402.2 51.8 all-reduce.4
where the time goes:
time: 506 us; the launch traced here: 505 us
  waiting for transfers between devices  303 us (60%)
  other arithmetic  76 us (15%)
  matrix products  44.5 us (9%)
  local copies, waits for them, and re-layouts  44 us (9%)
  starting transfers between devices  22.8 us (5%)
  between operations  14.8 us (3%)
    all_to_all x1, waiting for transfers between devices, per_device(): lax.all_to_all(to_buckets(head_rows, position, layout), 'rel', split_axis...  95.5 us
    psum x1, waiting for transfers between devices, broadcast(): return lax.psum(jnp.where(mine, shard, jnp.zeros_like(shard)), axis)  82.8 us
    all_to_all x1, waiting for transfers between devices, per_device(): lax.all_to_all(to_buckets(tail_rows, position, layout), 'rel', split_axis...  70.6 us
    scatter x2, other arithmetic, to_buckets(): filled = jnp.zeros(flat_shape, values.dtype).at[position].set(values)  50.3 us
    gather x2, local copies, waits for them, and re-layouts, from_buckets(): return stacked.reshape((-1,) + stacked.shape[3:])[position]  34.1 us
    psum x1, waiting for transfers between devices, per_device(): lax.psum(partial_value.astype(jnp.bfloat16), 'grp').astype(jnp.float32)  29.9 us
    all_to_all x1, waiting for transfers between devices, per_device(): lax.all_to_all(head_back, 'rel', split_axis=0, concat_axis=0, tiled=True)  23.6 us
    dot_general x1, matrix products, score_rows(): jnp.dot(query_rows, negatives.T, preferred_element_type=jnp.float32)  16.5 us
  transfers between devices with their start and end apart: 6, of which 5 were waited for; matrix products, arithmetic and copies ran while one was open for 19% of the time, Pallas kernels for 0%

commit v1 on v0

--- a/solution.py
+++ b/solution.py
@@ -4,9 +4,47 @@
 from jax.sharding import PartitionSpec as P
 
 LEARNING_RATE = 1.0
+BF = jnp.bfloat16
+F32 = jnp.float32
 
 
 def broadcast(shard, axis, root):
+    mine = lax.axis_index(axis) == root
+    return lax.psum(jnp.where(mine, shard, jnp.zeros_like(shard)), axis)
+
+
+def one_hot(ids, count):
+    return (ids[:, None] == jnp.arange(count, dtype=jnp.int32)[None, :]).astype(BF)
+
+
+def select_rows(selector, rows):
+    return jnp.dot(selector, rows, preferred_element_type=F32).astype(BF)
+
+
+def select_back(selector, rows):
+    return lax.dot_general(
+        selector, rows, (((0,), (0,)), ((), ())), preferred_element_type=F32
+    ).astype(BF)
+
+
+def score_rows(query_rows, tail_rows, negatives):
+    positive = jnp.sum(query_rows.astype(F32) * tail_rows.astype(F32), axis=-1)
+    neg_scores = lax.dot_general(
+        query_rows, negatives, (((1,), (1,)), ((), ())), preferred_element_type=F32
+    )
+    losses = jax.nn.softplus(-positive) + jnp.mean(jax.nn.softplus(neg_scores), axis=-1)
+    coefs = (jax.nn.sigmoid(neg_scores) / negatives.shape[0]).astype(BF)
+    grad_query = -jax.nn.sigmoid(-positive)[:, None] * tail_rows.astype(F32)
+    grad_query = grad_query + jnp.dot(coefs, negatives, preferred_element_type=F32)
+    return (losses.astype(BF), grad_query.astype(BF))
+
+
+def adagrad(weight, accumulator, gradient):
+    new_accum = accumulator + jnp.mean(gradient * gradient, axis=-1)
+    return (weight - LEARNING_RATE * gradient / jnp.sqrt(new_accum)[..., None], new_accum)
+
+
+def broadcast_rows(shard, axis, root):
     mine = lax.axis_index(axis) == root
     return lax.psum(jnp.where(mine, shard, jnp.zeros_like(shard)), axis)
 
@@ -17,7 +55,7 @@
     return jnp.sum(one_hot * running, axis=-1)
 
 
-def score_rows(query_rows, tail_rows, negatives):
+def score_rows_rows(query_rows, tail_rows, negatives):
     positive = jnp.sum(query_rows.astype(jnp.float32) * tail_rows.astype(jnp.float32), axis=-1)
     neg_scores = jnp.dot(query_rows, negatives.T, preferred_element_type=jnp.float32)
     losses = jax.nn.softplus(-positive) + jnp.mean(jax.nn.softplus(neg_scores), axis=-1)
@@ -27,7 +65,7 @@
     return (losses.astype(jnp.bfloat16), grad_query.astype(jnp.bfloat16))
 
 
-def adagrad(weight, accumulator, gradient):
+def adagrad_rows(weight, accumulator, gradient):
     new_accum = accumulator + jnp.mean(gradient * gradient, axis=-1)
     return (weight - LEARNING_RATE * gradient / jnp.sqrt(new_accum)[..., None], new_accum)
 
@@ -42,7 +80,7 @@
     return stacked.reshape((-1,) + stacked.shape[3:])[position]
 
 
-def per_device(head_ids, relations, tail_ids, neg_owner, entities, rel_weight, rel_accum):
+def per_device_rows(head_ids, relations, tail_ids, neg_owner, entities, rel_weight, rel_accum):
     rows_here = head_ids.shape[0]
     width = entities.shape[1]
     owner_count = lax.axis_size("rel")
@@ -54,7 +92,7 @@
     head_rows = jnp.take(entities, head_ids, axis=0)
     tail_rows = jnp.take(entities, tail_ids, axis=0)
     matrices = rel_weight.astype(jnp.bfloat16)
-    negatives = broadcast(entities, ("grp", "rel"), neg_owner[0])
+    negatives = broadcast_rows(entities, ("grp", "rel"), neg_owner[0])
     held_rows, held_tails = (
         lax.all_to_all(
             to_buckets(head_rows, position, layout), "rel", split_axis=0, concat_axis=0, tiled=True
@@ -66,7 +104,7 @@
     projected = jnp.einsum(
         "srcd,rde->srce", held_rows, matrices, preferred_element_type=jnp.float32
     ).astype(jnp.bfloat16)
-    slot_losses, slot_grads = score_rows(
+    slot_losses, slot_grads = score_rows_rows(
         projected.reshape(-1, width), held_tails.reshape(-1, width), negatives
     )
     grad_rows = slot_grads.reshape(held_rows.shape)
@@ -84,8 +122,67 @@
     head_grad = from_buckets(back_grads, position)
     losses = from_buckets(back_losses, position)
     summed = lax.psum(partial_value.astype(jnp.bfloat16), "grp").astype(jnp.float32)
+    new_rel, new_accum = adagrad_rows(rel_weight, rel_accum, summed)
+    return (losses, head_grad, new_rel, new_accum)
+
+
+def per_device(head_ids, relations, tail_ids, neg_owner, entities, rel_weight, rel_accum):
+    rows_here = head_ids.shape[0]
+    width = entities.shape[1]
+    shard_rows = entities.shape[0]
+    owner_count = lax.axis_size("rel")
+    local_rels = rel_weight.shape[0]
+    rel_count = owner_count * local_rels
+    capacity = 2 * rows_here // rel_count
+    slots = rel_count * capacity
+
+    half = local_rels // 2
+    core = lax.axis_index("core")
+    mine = lax.dynamic_slice_in_dim(rel_weight, core * half, half, 0).astype(BF)
+    matrices = lax.all_gather(mine, "rel", axis=0, tiled=False)
+    matrices = lax.all_gather(matrices, "core", axis=1, tiled=False)
+    matrices = matrices.reshape(rel_count, width, width)
+    negatives = broadcast(entities, ("x", "core", "rel"), neg_owner[0])
+
+    rel_ids = relations[:, 0]
+    rel_hot = one_hot(rel_ids, rel_count)
+    order = jnp.arange(rows_here, dtype=jnp.int32)
+    lower = (order[:, None] >= order[None, :]).astype(BF)
+    running = jnp.dot(lower, rel_hot, preferred_element_type=F32)
+    rank = jnp.sum(running * rel_hot.astype(F32), axis=-1).astype(jnp.int32) - 1
+    position = rel_ids * capacity + rank
+    bucket = (jnp.arange(slots, dtype=jnp.int32)[:, None] == position[None, :]).astype(BF)
+
+    head_rows = select_rows(one_hot(head_ids, shard_rows), entities)
+    tail_rows = select_rows(one_hot(tail_ids, shard_rows), entities)
+    held_rows = select_rows(bucket, head_rows).reshape(rel_count, capacity, width)
+
+    projected = jnp.einsum(
+        "rcd,rde->rce", held_rows, matrices, preferred_element_type=F32
+    ).astype(BF)
+    query_rows = select_back(bucket, projected.reshape(slots, width))
+    losses, grad_query = score_rows(query_rows, tail_rows, negatives)
+    grad_rows = select_rows(bucket, grad_query).reshape(rel_count, capacity, width)
+
+    partial_value = jnp.einsum(
+        "rcd,rce->rde", held_rows, grad_rows, preferred_element_type=F32
+    ).astype(BF)
+    partial_value = partial_value.reshape(owner_count, 2, half, width, width)
+    summed = lax.psum_scatter(partial_value, "core", scatter_dimension=1, tiled=True)
+    summed = lax.psum_scatter(summed, "rel", scatter_dimension=0, tiled=True)
+    summed = lax.psum(summed.reshape(half, width, width), "x")
+    summed = lax.all_gather(summed, "core", axis=0, tiled=True).astype(F32)
+
+    head_back = jnp.einsum(
+        "rce,rde->rcd", grad_rows, matrices, preferred_element_type=F32
+    ).astype(BF)
+    head_grad = select_back(bucket, head_back.reshape(slots, width))
+
     new_rel, new_accum = adagrad(rel_weight, rel_accum, summed)
     return (losses, head_grad, new_rel, new_accum)
+
+
+GATHER_LIMIT = 16 * 1024 * 1024
 
 
 def solution(mesh):
@@ -98,15 +195,34 @@
         P("rel", None, None),
         P("rel", None),
     )
-    return jax.shard_map(
+    outs = (
+        P(("grp", "rel")),
+        P(("grp", "rel"), None),
+        P("rel", None, None),
+        P("rel", None),
+    )
+    rows_step = jax.shard_map(
+        per_device_rows, mesh=mesh, in_specs=placed, out_specs=outs, check_vma=False
+    )
+    groups, owners = mesh.devices.shape
+    split = jax.sharding.Mesh(mesh.devices.reshape(groups // 2, 2, owners), ("x", "core", "rel"))
+
+    def respec(spec):
+        return P(*[("x", "core", "rel") if part == ("grp", "rel") else part for part in spec])
+
+    local_step = jax.shard_map(
         per_device,
-        mesh=mesh,
-        in_specs=placed,
-        out_specs=(
-            P(("grp", "rel")),
-            P(("grp", "rel"), None),
-            P("rel", None, None),
-            P("rel", None),
-        ),
+        mesh=split,
+        in_specs=tuple(respec(s) for s in placed),
+        out_specs=tuple(respec(s) for s in outs),
         check_vma=False,
     )
+
+    def step(head_ids, relations, tail_ids, neg_owner, entities, rel_weight, rel_accum):
+        args = (head_ids, relations, tail_ids, neg_owner, entities, rel_weight, rel_accum)
+        width = rel_weight.shape[-1]
+        if rel_weight.shape[0] * width * width * 2 <= GATHER_LIMIT:
+            return local_step(*args)
+        return rows_step(*args)
+
+    return step

time: 506 us -> 626 us (1.24); the launches traced: 505 us -> 616 us
  waiting for transfers between devices: 303 us -> 476 us
  other arithmetic: 76 us -> 9.88 us
  matrix products: 44.5 us -> 100 us
  local copies, waits for them, and re-layouts: 44 us -> 13.6 us
  starting transfers between devices: 22.8 us -> 0.29 us
    all_to_all x4 -> x0, waiting for transfers between devices: 190 us -> none  [the longest x1 95.5 us: per_device(): lax.all_to_all(to_buckets(head_rows, position, layout), 'rel', split_axis...]
    reduce_scatter x0 -> x1, waiting for transfers between devices: none -> 149 us  [per_device(): summed = lax.psum_scatter(summed, 'rel', scatter_dimension=0, tiled=True)]
    all_gather x0 -> x3, waiting for transfers between devices: none -> 141 us  [the longest x1 128 us: per_device(): matrices = lax.all_gather(mine, 'rel', axis=0, tiled=False)]
    unnamed x2 -> x8, waiting for transfers between devices: 0.03 us -> 59 us
    dot_general x5 -> x11, matrix products: 44.5 us -> 100 us  [the longest x4 37.5 us: select_rows(): return jnp.dot(selector, rows, preferred_element_type=F32).astype(BF)]
    scatter x2 -> x0, other arithmetic: 50.3 us -> none  [to_buckets(): filled = jnp.zeros(flat_shape, values.dtype).at[position].set(values)]
    gather x2 -> x0, local copies, waits for them, and re-layouts: 34.1 us -> none  [from_buckets(): return stacked.reshape((-1,) + stacked.shape[3:])[position]]
    all_to_all x4 -> x0, starting transfers between devices: 22.5 us -> none  [the longest x1 7.44 us: per_device(): lax.all_to_all(to_buckets(tail_rows, position, layout), 'rel', split_axis...]
  transfers between devices with their start and end apart: 6 -> 7, of which waited for: 5 -> 6; matrix products, arithmetic and copies ran while one was open for 19% -> 10% of each run, Pallas kernels for 0% -> 0%
where the time goes in v1:
time: 626 us; the launch traced here: 616 us
  waiting for transfers between devices  476 us (76%)
  matrix products  100 us (16%)
  between operations  16.5 us (3%)
  local copies, waits for them, and re-layouts  13.6 us (2%)
  other arithmetic  9.88 us (2%)
    reduce_scatter x1, waiting for transfers between devices, per_device(): summed = lax.psum_scatter(summed, 'rel', scatter_dimension=0, tiled=True)  149 us
    all_gather x1, waiting for transfers between devices, per_device(): matrices = lax.all_gather(mine, 'rel', axis=0, tiled=False)  128 us
    psum x1, waiting for transfers between devices, broadcast(): return lax.psum(jnp.where(mine, shard, jnp.zeros_like(shard)), axis)  88.3 us
    unnamed x8, waiting for transfers between devices  59 us
    psum x1, waiting for transfers between devices, per_device(): summed = lax.psum(summed.reshape(half, width, width), 'x')  39.1 us
    dot_general x4, matrix products, select_rows(): return jnp.dot(selector, rows, preferred_element_type=F32).astype(BF)  37.5 us
    dot_general x2, matrix products, select_back(): lax.dot_general(selector, rows, (((0,), (0,)), ((), ())), preferred_eleme...  19.4 us
    all_gather x1, waiting for transfers between devices, per_device(): matrices = lax.all_gather(matrices, 'core', axis=1, tiled=False)  12.9 us
  transfers between devices with their start and end apart: 7, of which 6 were waited for; matrix products, arithmetic and copies ran while one was open for 10% of the time, Pallas kernels for 0%

profile of v1, /device:TPU:0, one launch (start us, length us, event | category | flops | bytes accessed | tf_op | source)
XLA Modules:
  0.0 616.5 jit_solution(17975725279980683553)
XLA Ops:
  8.0 0.0 all-gather.8.cloned.1.call-start
  8.0 2.7 dynamic-slice_convert_fusion
  10.7 0.0 all-gather.8.cloned.1.call-update
  10.8 0.0 all-gather.10.cloned.1.call-start
  10.8 127.9 %all-gather.8.cloned.1.call-done = bf16[16,512,512]{2,1,0:T(8,128)(2,1)} async-done(((bf16[2,512,512]{2,1,0:T(8,128)(2,1)}), bf16[16,512,512]{2,1,0:T(8,128)(2,1)}) %all-gather.8.cloned.1.call-update) | async-done | bytes 8388624 | tf_op jit(solution)/shard_map/all_gather | solution.py:142
  138.7 0.0 copy-start
  138.7 0.0 copy-start.1
  138.7 0.0 all-gather.10.cloned.1.call-update
  138.8 0.0 all-reduce.5.cloned.1.call-start
  139.5 0.4 copy-done
  140.0 1.1 broadcast_select_fusion
  141.1 0.0 copy-start.4
  141.1 0.0 all-reduce.5.cloned.1.call-update
  141.1 0.0 all-reduce.9.cloned.1.call-start
  141.1 0.0 copy-done.1
  141.1 1.5 fusion.27
  142.7 0.0 copy-done.4
  142.7 2.6 fusion.62
  145.3 10.4 %fusion.12 = bf16[4096,512]{1,0:T(8,128)(2,1)} fusion(s32[2048]{0:T(1024)S(1)} %add_add_fusion, bf16[2048,512]{1,0:T(8,128)(2,1)S(1)} %fusion.62), kind=kOutput, calls=%fused_computation.19 | convolution fusion | flops 8600420352 | bytes 6299648 | tf_op jit(solution)/shard_map/dot_general | solution.py:21
  155.7 12.9 %all-gather.10.cloned.1.call-done = bf16[8,4,512,512]{3,2,1,0:T(8,128)(2,1)} async-done(((bf16[8,2,512,512]{3,2,1,0:T(8,128)(2,1)}), bf16[8,4,512,512]{3,2,1,0:T(8,128)(2,1)}) %all-gather.10.cloned.1.call-update) | async-done | bytes 16777232 | tf_op jit(solution)/shard_map/all_gather | solution.py:143
  168.6 9.5 %convolution_convert_fusion.2 = bf16[32,128,512]{2,1,0:T(8,128)(2,1)S(1)} fusion(bf16[32,128,512]{2,1,0:T(8,128)(2,1)} %bitcast.50, bf16[32,512,512]{2,1,0:T(8,128)(2,1)} %bitcast.45), kind=kOutput, calls=%fused_computation.38 | convolution fusion | flops 2149580800 | bytes 25165824 | tf_op jit(solution)/shard_map/rcd,rde->rce/dot_general | solution.py:160
  178.1 0.0 copy-start.5
  178.1 9.4 %fusion.22 = bf16[2048,512]{0,1:T(8,128)(2,1)S(1)} fusion(bf16[4096,512]{1,0:T(8,128)(2,1)S(1)} %bitcast.53, s32[2048]{0:T(1024)S(1)} %add_add_fusion), kind=kOutput, calls=%fused_computation.33 | convolution fusion | flops 8599371776 | bytes 6299648 | tf_op jit(solution)/shard_map/dot_general | solution.py:25
  187.5 0.0 copy-start.7
  187.5 1.4 copy-done.7
  188.8 0.0 copy-done.5
  188.8 4.1 fusion.14
  192.9 88.3 %all-reduce.5.cloned.1.call-done = bf16[1024,512]{1,0:T(8,128)(2,1)} async-done(((bf16[1024,512]{1,0:T(8,128)(2,1)}), bf16[1024,512]{1,0:T(8,128)(2,1)}) %all-reduce.5.cloned.1.call-update) | async-done | bytes 1048592 | tf_op jit(solution)/shard_map/psum | solution.py:13
  281.2 0.0 copy-start.3
  281.2 10.7 %fusion.9 = (f32[2048]{0:T(1024)S(1)}, f32[2048,1024]{0,1:T(8,128)}) fusion(bf16[1024,512]{1,0:T(8,128)(2,1)} %all-reduce.5.cloned.1.call-done, bf16[2048,512]{0,1:T(8,128)(2,1)} %copy-done.7), kind=kOutput, calls=%fused_computation.13 | convolution fusion | flops 2162161664 | bytes 11542528 | tf_op jit(solution)/shard_map/dot_general | solution.py:32
  291.9 0.6 divide_negate_fusion
  292.5 0.0 copy-done.3
  292.5 20.4 %fusion.13 = bf16[4096,512]{1,0:T(8,128)(2,1)} fusion(s32[2048]{0:T(1024)S(1)} %add_add_fusion, bf16[2048,512]{0,1:T(8,128)(2,1)} %get-tuple-element.9, bf16[1024,512]{1,0:T(8,128)(2,1)S(1)} %copy-done.3, f32[2048,1024]{0,1:T(8,128)} %get-tuple-element.11, f32[2048]{0:T(1024)S(1)} %get-tuple-element.6), kind=kOutput, calls=%fused_computation.20 | convolution fusion | flops 10762584064 | bytes 15745024 | tf_op jit(solution)/shard_map/dot_general | solution.py:21
  313.0 10.9 %convolution_convert_fusion = bf16[32,512,512]{2,1,0:T(8,128)(2,1)} fusion(bf16[32,128,512]{2,1,0:T(8,128)(2,1)} %bitcast.51, bf16[32,128,512]{2,1,0:T(8,128)(2,1)} %bitcast.48), kind=kOutput, calls=%fused_computation.12 | convolution fusion | flops 2155872256 | bytes 25165824 | tf_op jit(solution)/shard_map/rcd,rce->rde/dot_general | solution.py:167
  323.9 0.0 copy-start.6
  323.9 0.0 all-reduce.9.cloned.1.call-update
  323.9 0.0 reduce-scatter.5.cloned.1.call-start
  323.9 0.6 copy-done.6
  324.5 0.6 dynamic-slice
  325.1 58.9 %all-reduce.9.cloned.1.call-done = bf16[8,2,2,512,512]{4,3,2,1,0:T(8,128)(2,1)} async-done(((bf16[8,2,2,512,512]{4,3,2,1,0:T(8,128)(2,1)}), bf16[8,2,2,512,512]{4,3,2,1,0:T(8,128)(2,1)}) %all-reduce.9.cloned.1.call-update) | async-done | bytes 16777232
  384.0 8.0 %constant_dynamic-slice_fusion = bf16[8,1,2,512,512]{4,3,2,1,0:T(8,128)(2,1)} fusion(bf16[8,2,2,512,512]{4,3,2,1,0:T(8,128)(2,1)} %all-reduce.9.cloned.1.call-done, u32[]{:T(128)} %bitcast.16), kind=kLoop, calls=%fused_computation.52 | loop fusion | bytes 16777220
  392.0 0.0 reduce-scatter.5.cloned.1.call-update
  392.0 0.0 all-reduce.7.cloned.1.call-start
  392.0 148.8 %reduce-scatter.5.cloned.1.call-done = bf16[1,1,2,512,512]{4,3,2,1,0:T(8,128)(2,1)} async-done(((bf16[8,1,2,512,512]{4,3,2,1,0:T(8,128)(2,1)}), bf16[1,1,2,512,512]{4,3,2,1,0:T(8,128)(2,1)}) %reduce-scatter.5.cloned.1.call-update) | async-done | bytes 1048592 | tf_op jit(solution)/shard_map/reduce_scatter | solution.py:172
  540.8 0.0 all-reduce.7.cloned.1.call-update
  540.8 0.0 all-gather.6.cloned.1.call-start
  540.9 39.1 %all-reduce.7.cloned.1.call-done = bf16[2,512,512]{2,1,0:T(8,128)(2,1)} async-done(((bf16[2,512,512]{2,1,0:T(8,128)(2,1)}), bf16[2,512,512]{2,1,0:T(8,128)(2,1)}) %all-reduce.7.cloned.1.call-update) | async-done | bytes 1048592 | tf_op jit(solution)/shard_map/psum | solution.py:173
  580.0 0.0 all-gather.6.cloned.1.call-update
  580.0 10.6 %convolution_convert_fusion.1 = bf16[32,128,512]{2,1,0:T(8,128)(2,1)S(1)} fusion(bf16[32,128,512]{2,1,0:T(8,128)(2,1)} %bitcast.49, bf16[32,512,512]{2,1,0:T(8,128)(2,1)} %bitcast.46), kind=kOutput, calls=%fused_computation.37 | convolution fusion | flops 2149580800 | bytes 25165824 | tf_op jit(solution)/shard_map/rce,rde->rcd/dot_general | solution.py:176
  590.7 0.0 copy-start.2
  590.7 10.1 %fusion.23 = bf16[2048,512]{1,0:T(8,128)(2,1)} fusion(bf16[4096,512]{1,0:T(8,128)(2,1)S(1)} %bitcast.52, s32[2048]{0:T(1024)S(1)} %add_add_fusion), kind=kOutput, calls=%fused_computation.34 | convolution fusion | flops 8599371776 | bytes 6299648 | tf_op jit(solution)/shard_map/dot_general | solution.py:25
  600.7 0.0 all-gather.6.cloned.1.call-done
  600.7 2.1 fusion.17
  602.8 0.0 copy-done.2
  602.8 0.6 fusion.36
  603.4 5.5 fusion.18
  (1 shorter events, 0.0 us)
Async XLA Ops:
  8.0 130.7 %all-gather.8.cloned.1.call-start = ((), (), s32[]{:S(2)}) async-start(), calls=%async_computation.5 | async-start | bytes 9437184 | tf_op jit(solution)/shard_map/all_gather | solution.py:142
  10.8 157.8 %all-gather.10.cloned.1.call-start = ((), (), s32[]{:S(2)}) async-start(), calls=%async_computation.6 | async-start | bytes 25165824 | tf_op jit(solution)/shard_map/all_gather | solution.py:143
  138.7 1.2 copy-start
  138.7 2.4 copy-start.1
  138.8 142.4 %all-reduce.5.cloned.1.call-start = ((), (), s32[]{:S(2)}) async-start(), calls=%async_computation.1 | async-start | bytes 2097152 | tf_op jit(solution)/shard_map/psum | solution.py:13
  141.1 1.6 copy-start.4
  141.1 242.9 %all-reduce.9.cloned.1.call-start = ((), (), s32[]{:S(2)}) async-start(), calls=%async_computation.7 | async-start | bytes 33554432
  178.1 10.8 %copy-start.5 = (s32[2048]{0:T(1024)S(1)}, s32[2048]{0:T(1024)}, u32[]{:S(2)}) copy-start(s32[2048]{0:T(1024)} %param.9) | copy-start | bytes 24580
  187.5 1.4 copy-start.7
  281.2 11.3 %copy-start.3 = (bf16[1024,512]{1,0:T(8,128)(2,1)S(1)}, bf16[1024,512]{1,0:T(8,128)(2,1)}, u32[]{:S(2)}) copy-start(bf16[1024,512]{1,0:T(8,128)(2,1)} %all-reduce.5.cloned.1.call-done) | copy-start | bytes 3145732
  323.9 0.7 copy-start.6
  323.9 216.9 %reduce-scatter.5.cloned.1.call-start = ((), (), s32[]{:S(2)}) async-start(), calls=%async_computation.2 | async-start | bytes 9437184 | tf_op jit(solution)/shard_map/reduce_scatter | solution.py:172
  392.0 188.0 %all-reduce.7.cloned.1.call-start = ((), (), s32[]{:S(2)}) async-start(), calls=%async_computation.3 | async-start | bytes 2097152 | tf_op jit(solution)/shard_map/psum | solution.py:173
  540.8 59.9 %all-gather.6.cloned.1.call-start = ((), (), s32[]{:S(2)}) async-start(), calls=%async_computation.4 | async-start | bytes 3145728 | tf_op jit(solution)/shard_map/all_gather | solution.py:174
  590.7 12.2 %copy-start.2 = (f32[4,512]{1,0:T(4,128)S(1)}, f32[4,512]{1,0:T(4,128)}, u32[]{:S(2)}) copy-start(f32[4,512]{1,0:T(4,128)} %param.13) | copy-start | bytes 24580
Sparse Core Ops, SparseCore 0:
  11.5 127.1 all-gather.7
  140.3 28.2 all-gather.9
  324.0 59.9 all-reduce.8
  392.1 148.6 reduce-scatter.4
  580.1 10.5 all-gather.5
Sparse Core Ops, SparseCore 1:
  144.4 136.7 all-reduce.4
  540.9 39.0 all-reduce.6

commit v2 on v0

v2 whole, which is shorter than its diff:
```python
import jax
import jax.numpy as jnp
from jax import lax
from jax.sharding import PartitionSpec as P

LEARNING_RATE = 1.0


def broadcast(shard, axis, root):
    mine = lax.axis_index(axis) == root
    return lax.psum(jnp.where(mine, shard, jnp.zeros_like(shard)), axis)


def score_rows(query_rows, tail_rows, negatives):
    positive = jnp.sum(query_rows.astype(jnp.float32) * tail_rows.astype(jnp.float32), axis=-1)
    neg_scores = jnp.dot(query_rows, negatives.T, preferred_element_type=jnp.float32)
    losses = jax.nn.softplus(-positive) + jnp.mean(jax.nn.softplus(neg_scores), axis=-1)
    coefs = (jax.nn.sigmoid(neg_scores) / negatives.shape[0]).astype(jnp.bfloat16)
    grad_query = -jax.nn.sigmoid(-positive)[:, None] * tail_rows.astype(jnp.float32)
    grad_query = grad_query + jnp.dot(coefs, negatives, preferred_element_type=jnp.float32)
    return (losses.astype(jnp.bfloat16), grad_query.astype(jnp.bfloat16))


def adagrad(weight, accumulator, gradient):
    new_accum = accumulator + jnp.mean(gradient * gradient, axis=-1)
    return (weight - LEARNING_RATE * gradient / jnp.sqrt(new_accum)[..., None], new_accum)


def one_hot(ids, count):
    return (ids[:, None] == jnp.arange(count, dtype=jnp.int32)[None, :]).astype(jnp.bfloat16)


def select_rows(selector, rows):
    return jnp.dot(selector, rows, preferred_element_type=jnp.float32).astype(jnp.bfloat16)


def per_device(head_ids, relations, tail_ids, neg_owner, entities, rel_weight, rel_accum):
    rows_here = head_ids.shape[0]
    width = entities.shape[1]
    shard_rows = entities.shape[0]
    owner_count = lax.axis_size("rel")
    local_rels = rel_weight.shape[0]
    rel_count = owner_count * local_rels
    capacity = 2 * rows_here // rel_count
    layout = (owner_count, local_rels, capacity)
    slots = rel_count * capacity
    negatives = broadcast(entities, ("grp", "rel"), neg_owner[0])
    rel_ids = relations[:, 0]
    rel_hot = one_hot(rel_ids, rel_count)
    order = jnp.arange(rows_here, dtype=jnp.int32)
    lower = (order[:, None] >= order[None, :]).astype(jnp.bfloat16)
    running = jnp.dot(lower, rel_hot, preferred_element_type=jnp.float32)
    rank = jnp.sum(running * rel_hot.astype(jnp.float32), axis=-1).astype(jnp.int32) - 1
    position = rel_ids * capacity + rank
    ids = jnp.stack([head_ids, tail_ids], axis=-1) + 1
    slot_ids = jnp.zeros((slots, 2), jnp.int32).at[position].set(ids) - 1
    held_rows = select_rows(one_hot(slot_ids[:, 0], shard_rows), entities).reshape(layout + (width,))
    held_rows = lax.all_to_all(held_rows, "rel", split_axis=0, concat_axis=0, tiled=True)
    tail_send = select_rows(one_hot(slot_ids[:, 1], shard_rows), entities).reshape(layout + (width,))
    held_tails = lax.all_to_all(tail_send, "rel", split_axis=0, concat_axis=0, tiled=True)
    matrices = rel_weight.astype(jnp.bfloat16)
    projected = jnp.einsum(
        "srcd,rde->srce", held_rows, matrices, preferred_element_type=jnp.float32
    ).astype(jnp.bfloat16)
    slot_losses, slot_grads = score_rows(
        projected.reshape(-1, width), held_tails.reshape(-1, width), negatives
    )
    grad_rows = slot_grads.reshape(held_rows.shape)
    partial_value = jnp.einsum(
        "srcd,srce->rde", held_rows, grad_rows, preferred_element_type=jnp.float32
    )
    summed = lax.psum(partial_value.astype(jnp.bfloat16), "grp").astype(jnp.float32)
    head_back = jnp.einsum(
        "srce,rde->srcd", grad_rows, matrices, preferred_element_type=jnp.float32
    ).astype(jnp.bfloat16)
    per_owner = local_rels * capacity
    extra = -(-per_owner // width)
    loss_rows = slot_losses.reshape(owner_count, per_owner)
    loss_rows = jnp.pad(loss_rows, ((0, 0), (0, extra * width - per_owner)))
    loss_rows = loss_rows.reshape(owner_count, extra, width)
    packed = jnp.concatenate([head_back.reshape(owner_count, per_owner, width), loss_rows], axis=1)
    packed = lax.all_to_all(packed, "rel", split_axis=0, concat_axis=0, tiled=True)
    back_grads = packed[:, :per_owner].reshape(slots, width)
    back_losses = packed[:, per_owner:].reshape(owner_count, extra * width)
    back_losses = back_losses[:, :per_owner].reshape(slots)
    taken = one_hot(position, slots)
    head_grad = select_rows(taken, back_grads)
    losses = jnp.dot(taken, back_losses, preferred_element_type=jnp.float32).astype(jnp.bfloat16)
    new_rel, new_accum = adagrad(rel_weight, rel_accum, summed)
    return (losses, head_grad, new_rel, new_accum)


def solution(mesh):
    placed = (
        P(("grp", "rel")),
        P(("grp", "rel"), None),
        P(("grp", "rel")),
        P(),
        P(("grp", "rel"), None),
        P("rel", None, None),
        P("rel", None),
    )
    return jax.shard_map(
        per_device,
        mesh=mesh,
        in_specs=placed,
        out_specs=(
            P(("grp", "rel")),
            P(("grp", "rel"), None),
            P("rel", None, None),
            P("rel", None),
        ),
        check_vma=False,
    )
```

time: 506 us -> 499 us (0.986); the launches traced: 505 us -> 491 us
  other arithmetic: 76 us -> 18 us
  waiting for transfers between devices: 303 us -> 336 us
  matrix products: 44.5 us -> 77 us
  local copies, waits for them, and re-layouts: 44 us -> 20.5 us
    scatter x2 -> x0, other arithmetic: 50.3 us -> none  [to_buckets(): filled = jnp.zeros(flat_shape, values.dtype).at[position].set(values)]
    gather x2 -> x0, local copies, waits for them, and re-layouts: 34.1 us -> none  [from_buckets(): return stacked.reshape((-1,) + stacked.shape[3:])[position]]
    dot_general x0 -> x5, matrix products: none -> 31 us  [the longest x3 22.5 us: select_rows(): jnp.dot(selector, rows, preferred_element_type=jnp.float32)]
    psum x1, waiting for transfers between devices: 29.9 us -> 52.6 us  [per_device(): lax.psum(partial_value.astype(jnp.bfloat16), 'grp').astype(jnp.float32)]
    all_to_all x4 -> x3, waiting for transfers between devices: 190 us -> 200 us  [the longest x1 95.5 us: per_device(): lax.all_to_all(held_rows, 'rel', split_axis=0, concat_axis=0, tiled=True)]
    another operation x2 -> x0, other arithmetic: 9.27 us -> none
    psum x1, starting transfers between devices: 0.04 us -> 8.43 us  [per_device(): lax.psum(partial_value.astype(jnp.bfloat16), 'grp').astype(jnp.float32)]
    scatter x0 -> x1, local copies, waits for them, and re-layouts: none -> 6.1 us  [per_device(): slot_ids = jnp.zeros((slots, 2), jnp.int32).at[position].set(ids) - 1]
  transfers between devices with their start and end apart: 6 -> 5, of which waited for: 5 -> 5; matrix products, arithmetic and copies ran while one was open for 19% -> 8% of each run, Pallas kernels for 0% -> 0%
where the time goes in v2:
time: 499 us; the launch traced here: 491 us
  waiting for transfers between devices  336 us (67%)
  matrix products  77 us (15%)
  starting transfers between devices  25.2 us (5%)
  local copies, waits for them, and re-layouts  20.5 us (4%)
  other arithmetic  18 us (4%)
  between operations  15.1 us (3%)
    all_to_all x1, waiting for transfers between devices, per_device(): lax.all_to_all(held_rows, 'rel', split_axis=0, concat_axis=0, tiled=True)  95.5 us
    all_to_all x1, waiting for transfers between devices, per_device(): lax.all_to_all(tail_send, 'rel', split_axis=0, concat_axis=0, tiled=True)  87 us
    psum x1, waiting for transfers between devices, broadcast(): return lax.psum(jnp.where(mine, shard, jnp.zeros_like(shard)), axis)  82.8 us
    psum x1, waiting for transfers between devices, per_device(): lax.psum(partial_value.astype(jnp.bfloat16), 'grp').astype(jnp.float32)  52.6 us
    dot_general x3, matrix products, select_rows(): jnp.dot(selector, rows, preferred_element_type=jnp.float32)  22.5 us
    all_to_all x1, waiting for transfers between devices, per_device(): lax.all_to_all(packed, 'rel', split_axis=0, concat_axis=0, tiled=True)  17.6 us
    dot_general x1, matrix products, score_rows(): jnp.dot(query_rows, negatives.T, preferred_element_type=jnp.float32)  16.2 us
    dot_general x1, matrix products, score_rows(): jnp.dot(coefs, negatives, preferred_element_type=jnp.float32)  10.8 us
  transfers between devices with their start and end apart: 5, of which 5 were waited for; matrix products, arithmetic and copies ran while one was open for 8% of the time, Pallas kernels for 0%

profile of v2, /device:TPU:0, one launch (start us, length us, event | category | flops | bytes accessed | tf_op | source)
XLA Modules:
  0.0 491.4 jit_solution(8501658927828690532)
XLA Ops:
  7.2 0.0 copy-start.3
  7.2 0.0 copy-start.4
  7.2 0.0 copy-start.5
  7.2 2.3 fusion.29
  9.5 0.0 copy-done.3
  9.5 0.0 copy-done.4
  9.5 0.0 copy-done.5
  9.6 0.4 copy.56
  9.9 6.1 %scatter_custom_fusion = s32[4096,2]{1,0:T(8,128)S(1)} fusion(s32[2048]{0:T(1024)S(1)} %bitcast.78, s32[2048,2]{1,0:T(8,128)S(1)} %copy.56, s32[]{:T(128)} %constant.17.clone.1), kind=kCustom, calls=%fused_computation.47 | custom fusion | bytes 32772 | tf_op jit(solution)/shard_map/scatter | solution.py:56
  16.0 0.0 copy-start.2
  16.1 0.1 broadcast_add_fusion
  16.2 1.7 slice_reduce_fusion
  17.9 0.0 copy-done.2
  17.9 6.2 %fusion.13 = bf16[4096,512]{1,0:T(8,128)(2,1)} fusion(bf16[1024,512]{1,0:T(8,128)(2,1)S(1)} %copy-done.2, s32[4096]{0:T(1024)S(1)} %get-tuple-element.4), kind=kOutput, calls=%fused_computation.22 | convolution fusion | flops 4301258752 | bytes 5259264 | tf_op jit(solution)/shard_map/dot_general | solution.py:34
  24.2 7.3 %all-to-all-start.1 = ((bf16[8,4,128,512]{3,2,1,0:T(8,128)(2,1)}), bf16[8,4,128,512]{3,2,1,0:T(8,128)(2,1)}, u32[]{:S(2)}, u32[]{:S(2)}) async-start(bf16[8,4,128,512]{3,2,1,0:T(8,128)(2,1)} %bitcast.67), calls=%async_computation.1 | async-start | bytes 8388608 | tf_op jit(solution)/shard_map/all_to_all | solution.py:60
  31.5 6.2 %fusion.14 = bf16[4096,512]{1,0:T(8,128)(2,1)} fusion(bf16[1024,512]{1,0:T(8,128)(2,1)S(1)} %copy-done.2, s32[4096]{0:T(1024)S(1)} %get-tuple-element.5), kind=kOutput, calls=%fused_computation.23 | convolution fusion | flops 4301258752 | bytes 5259264 | tf_op jit(solution)/shard_map/dot_general | solution.py:34
  37.7 87.0 %all-to-all-done.1 = bf16[8,4,128,512]{3,2,1,0:T(8,128)(2,1)} async-done(((bf16[8,4,128,512]{3,2,1,0:T(8,128)(2,1)}), bf16[8,4,128,512]{3,2,1,0:T(8,128)(2,1)}, u32[]{:S(2)}, u32[]{:S(2)}) %all-to-all-start.1) | async-done | bytes 4194336 | tf_op jit(solution)/shard_map/all_to_all | solution.py:60
  124.8 4.6 all-to-all-start
  129.4 0.3 all-reduce.3.cloned.1.call-start
  130.3 1.0 broadcast_select_fusion
  131.4 0.0 all-reduce.3.cloned.1.call-update
  131.4 95.5 %all-to-all-done = bf16[8,4,128,512]{3,2,1,0:T(8,128)(2,1)} async-done(((bf16[8,4,128,512]{3,2,1,0:T(8,128)(2,1)}), bf16[8,4,128,512]{3,2,1,0:T(8,128)(2,1)}, u32[]{:S(2)}, u32[]{:S(2)}) %all-to-all-start) | async-done | bytes 4194336 | tf_op jit(solution)/shard_map/all_to_all | solution.py:58
  226.9 7.2 %multiply_reduce_fusion = (f32[8,4,128]{2,0,1:T(8,128)S(1)}, bf16[8,4,128,512]{3,2,0,1:T(8,128)(2,1)S(1)}) fusion(bf16[8,4,128,512]{3,2,1,0:T(8,128)(2,1)} %all-to-all-done.1, f32[4,512,512]{2,1,0:T(8,128)} %param.12, bf16[8,4,128,512]{3,2,1,0:T(8,128)(2,1)} %all-to-all-done), kind=kOutput, calls=%fused_computation.18 | convolution fusion | flops 2159013888 | bytes 16793600 | tf_op jit(solution)/shard_map/srcd,rde->srce/dot_general | solution.py:62
  234.0 2.5 copy.61
  236.5 3.4 copy_convert_fusion
  239.9 4.2 copy.60
  244.2 82.8 %all-reduce.3.cloned.1.call-done = bf16[1024,512]{1,0:T(8,128)(2,1)} async-done(((bf16[1024,512]{1,0:T(8,128)(2,1)}), bf16[1024,512]{1,0:T(8,128)(2,1)}) %all-reduce.3.cloned.1.call-update) | async-done | bytes 1048592 | tf_op jit(solution)/shard_map/psum | solution.py:11
  327.0 0.0 copy-start
  327.0 0.0 copy-start.7
  327.0 16.2 %fusion.2 = (f32[4096]{0:T(1024)S(1)}, f32[4096,1024]{0,1:T(8,128)}) fusion(bf16[4096,512]{1,0:T(8,128)(2,1)} %bitcast.66, bf16[1024,512]{1,0:T(8,128)(2,1)} %all-reduce.3.cloned.1.call-done), kind=kOutput, calls=%fused_computation.5 | convolution fusion | flops 4324323328 | bytes 22036480 | tf_op jit(solution)/shard_map/dot_general | solution.py:16
  343.2 0.0 copy-done
  343.2 0.0 copy-done.7
  343.2 0.0 copy-start.1
  343.2 10.8 %fusion.9 = bf16[4096,512]{1,0:T(8,128)(2,1)} fusion(f32[8,4,128,512]{3,2,1,0:T(8,128)S(1)} %copy-done, bf16[1024,512]{1,0:T(8,128)(2,1)S(1)} %copy-done.7, f32[4096,1024]{0,1:T(8,128)} %get-tuple-element.11, f32[4096]{0:T(1024)S(1)} %bitcast.70), kind=kOutput, calls=%fused_computation.17 | convolution fusion | flops 4322230272 | bytes 30425088 | tf_op jit(solution)/shard_map/dot_general | solution.py:20
  354.0 0.0 copy-done.1
  354.0 4.6 convert_bitcast_fusion
  358.6 2.2 copy.63
  361.0 4.6 pad_maximum_fusion
  365.5 4.6 all-to-all-start.2
  370.1 8.4 %all-reduce.5.cloned.1.call-start = ((), (), s32[]{:S(2)}) async-start(), calls=%async_computation.4 | async-start | bytes 4194304 | tf_op jit(solution)/shard_map/psum | solution.py:72
  378.5 7.2 %bitcast_convert_fusion = bf16[4,512,512]{2,1,0:T(8,128)(2,1)} fusion(bf16[8,4,128,512]{3,2,1,0:T(8,128)(2,1)} %all-to-all-done, bf16[8,4,128,512]{3,2,1,0:T(8,128)(2,1)} %bitcast.80), kind=kOutput, calls=%fused_computation.29 | convolution fusion | flops 2148532224 | bytes 10485760 | tf_op jit(solution)/shard_map/srcd,srce->rde/dot_general | solution.py:69
  385.7 0.0 copy-start.6
  385.7 0.0 all-reduce.5.cloned.1.call-update
  385.7 52.6 %all-reduce.5.cloned.1.call-done = bf16[4,512,512]{2,1,0:T(8,128)(2,1)} async-done(((bf16[4,512,512]{2,1,0:T(8,128)(2,1)}), bf16[4,512,512]{2,1,0:T(8,128)(2,1)}) %all-reduce.5.cloned.1.call-update) | async-done | bytes 2097168 | tf_op jit(solution)/shard_map/psum | solution.py:72
  438.3 2.1 fusion.15
  440.4 0.0 copy-done.6
  440.4 0.6 fusion.44
  441.0 5.5 %fusion.16 = f32[4,512,512]{2,1,0:T(8,128)} fusion(f32[4,512,512]{2,1,0:T(8,128)} %param.12, bf16[4,512,512]{2,1,0:T(8,128)(2,1)} %all-reduce.5.cloned.1.call-done, f32[4,512]{1,0:T(4,128)S(1)} %get-tuple-element.6), kind=kLoop, calls=%fused_computation.28 | loop fusion | flops 3145728 | bytes 10493952 | tf_op jit(solution)/shard_map/sub | solution.py:26
  446.5 17.6 %all-to-all-done.2 = bf16[8,513,512]{2,1,0:T(8,128)(2,1)} async-done(((bf16[8,513,512]{2,1,0:T(8,128)(2,1)}), bf16[8,513,512]{2,1,0:T(8,128)(2,1)}, u32[]{:S(2)}, u32[]{:S(2)}) %all-to-all-start.2) | async-done | bytes 4202528 | tf_op jit(solution)/shard_map/all_to_all | solution.py:82
  464.1 2.5 slice.19
  466.6 10.1 %fusion.21 = bf16[2048,512]{1,0:T(8,128)(2,1)} fusion(bf16[4096,512]{1,0:T(8,128)(2,1)S(1)} %bitcast.68, s32[2048]{0:T(1024)S(1)} %bitcast.76), kind=kOutput, calls=%fused_computation.37 | convolution fusion | flops 8599371776 | bytes 6299648 | tf_op jit(solution)/shard_map/dot_general | solution.py:34
  476.6 0.8 slice.18
  477.5 6.2 %fusion.1 = f32[1,2048]{1,0:T(1,128)S(1)} fusion(bf16[4096,1]{0,1:T(2,128)(2,1)S(1)} %bitcast.71, s32[2048]{0:T(1024)S(1)} %bitcast.77), kind=kOutput, calls=%fused_computation.4 | convolution fusion | flops 25165824 | bytes 24576 | tf_op jit(solution)/shard_map/dot_general | solution.py:88
  483.7 0.6 convert_element_type.102
  (9 shorter events, 0.1 us)
Async XLA Ops:
  7.2 2.3 copy-start.3
  7.2 2.3 copy-start.4
  7.2 2.3 copy-start.5
  16.0 1.9 copy-start.2
  24.2 100.6 %all-to-all-start.1 = ((bf16[8,4,128,512]{3,2,1,0:T(8,128)(2,1)}), bf16[8,4,128,512]{3,2,1,0:T(8,128)(2,1)}, u32[]{:S(2)}, u32[]{:S(2)}) async-start(bf16[8,4,128,512]{3,2,1,0:T(8,128)(2,1)} %bitcast.67), calls=%async_computation.1 | async-start | bytes 8388608 | tf_op jit(solution)/shard_map/all_to_all | solution.py:60
  124.8 102.1 %all-to-all-start = ((bf16[8,4,128,512]{3,2,1,0:T(8,128)(2,1)}), bf16[8,4,128,512]{3,2,1,0:T(8,128)(2,1)}, u32[]{:S(2)}, u32[]{:S(2)}) async-start(bf16[8,4,128,512]{3,2,1,0:T(8,128)(2,1)} %bitcast.65), calls=%async_computation | async-start | bytes 8388608 | tf_op jit(solution)/shard_map/all_to_all | solution.py:58
  129.4 197.6 %all-reduce.3.cloned.1.call-start = ((), (), s32[]{:S(2)}) async-start(), calls=%async_computation.3 | async-start | bytes 2097152 | tf_op jit(solution)/shard_map/psum | solution.py:11
  327.0 16.2 %copy-start = (f32[8,4,128,512]{3,2,1,0:T(8,128)S(1)}, f32[8,4,128,512]{3,2,1,0:T(8,128)}, u32[]{:S(2)}) copy-start(f32[8,4,128,512]{3,2,1,0:T(8,128)} %copy.60) | copy-start | bytes 25165828
  327.0 16.2 %copy-start.7 = (bf16[1024,512]{1,0:T(8,128)(2,1)S(1)}, bf16[1024,512]{1,0:T(8,128)(2,1)}, u32[]{:S(2)}) copy-start(bf16[1024,512]{1,0:T(8,128)(2,1)} %all-reduce.3.cloned.1.call-done) | copy-start | bytes 3145732
  343.2 10.8 %copy-start.1 = (f32[4,512,512]{2,1,0:T(8,128)S(1)}, f32[4,512,512]{2,1,0:T(8,128)}, u32[]{:S(2)}) copy-start(f32[4,512,512]{2,1,0:T(8,128)} %param.12) | copy-start | bytes 12582916
  365.5 98.6 %all-to-all-start.2 = ((bf16[8,513,512]{2,1,0:T(8,128)(2,1)}), bf16[8,513,512]{2,1,0:T(8,128)(2,1)}, u32[]{:S(2)}, u32[]{:S(2)}) async-start(bf16[8,513,512]{2,1,0:T(8,128)(2,1)} %pad_maximum_fusion), calls=%async_computation.2 | async-start | bytes 8519680 | tf_op jit(solution)/shard_map/all_to_all | solution.py:82
  370.1 68.2 %all-reduce.5.cloned.1.call-start = ((), (), s32[]{:S(2)}) async-start(), calls=%async_computation.4 | async-start | bytes 4194304 | tf_op jit(solution)/shard_map/psum | solution.py:72
  385.7 54.7 %copy-start.6 = (f32[4,512]{1,0:T(4,128)S(1)}, f32[4,512]{1,0:T(4,128)}, u32[]{:S(2)}) copy-start(f32[4,512]{1,0:T(4,128)} %param.13) | copy-start | bytes 24580
Sparse Core Ops, SparseCore 0:
  135.9 190.9 all-reduce.2
  385.9 52.3 all-reduce.4
